TPU v7x, 256 devices: a whole 4x4x8 slice. The times are simulated.
256 devices in a mesh: section: 2 (over core), tok: 32 (over z, y), rep: 4 (over x).
Axes of the slice: x: 4, y: 4, z: 8, core: 2. Of those that a mesh axis runs over, the one named last changes fastest.
Arguments:
- inputs: bfloat16 [2, 4096, 1024], P(None, 'tok')
- segment_ids: int32 [2, 4096], replicated, may hold values from 0 to 7, as said below
- picks: int32 [2, 4096, 2], P(None, 'tok'), may hold values from 0 to 15, all different within a row; in each aligned block of 128 rows (0 to 127, 128 to 255, ..., all dimensions but the last counted through in order) at most 20 rows name the same one
- page_table: int32 [2, 32], replicated, may hold values from 0 to 31, each once within a row
- norm_gains: float32 [2, 2, 1024], P('section'), may hold values from 0.1 to 1.9
- attn_qkv: bfloat16 [2, 1024, 3, 1024], P('section', None, None, 'rep')
- attn_out: bfloat16 [2, 1024, 1024], P('section', 'rep'), may hold values from -0.1875 to 0.1875
- router: bfloat16 [2, 1024, 16], P('section')
- expert_in: bfloat16 [2, 32, 1024, 2, 1408], P('section', 'tok', None, None, 'rep'), may hold values from -0.1875 to 0.1875
- expert_out: bfloat16 [2, 32, 1408, 1024], P('section', 'tok', 'rep')
Outputs:
- layer_out: bfloat16 [2, 2, 4096, 1024], P('section', None, 'tok')
- kv_pages: bfloat16 [2, 2, 32, 128, 2, 1024], P('section', None, 'tok', None, None, 'rep')
Inputs may be any that keep to these rules, and one draw needn't show every extreme that they name: `picks`: within the tokens of one index of tok in one micro-batch, at most 20 tokens pick one expert, and some expert is picked by exactly 20. `segment_ids`: ids never fall along a micro-batch; every prompt has at least one token, a prompt spans at most 2048 tokens and one spans exactly 2048. `page_table`: each row is a permutation.
All inputs are finite; a program needn't handle non-finite values.
Results may differ from a plain program's by a relative error of at most 0.034.
Values may be sent and summed in bfloat16 or wider, within the bound.
No kernel may reach another device: no remote copies, remote signals or barrier semaphores. Data moves between devices by JAX's collectives and lax.ppermute only.
A program may use at most 128 MiB of HBM per device.

v0:
```python
import jax
import jax.numpy as jnp
from jax import lax
from jax.sharding import PartitionSpec as P

HEAD_DIM = 64
TOP = 2
PAGE = 128
CAP = 20
NEG_FILL = -1e30


def shifted(value, axis, steps):
    count = lax.axis_size(axis)
    first, last = (max(0, -steps), min(count, count - steps))
    return lax.ppermute(value, axis, [(source, source + steps) for source in range(first, last)])


def rms_scale(values, gains):
    return values * lax.rsqrt(jnp.mean(values * values, axis=-1, keepdims=True) + 1e-06) * gains


def attend(carry, queries, keys_vals, seg_query, pos_query, seg_key, pos_key):
    run_max, run_sum, run_acc = carry
    heads_here = run_acc.shape[0]
    head_size = run_acc.shape[2]
    rows_key = keys_vals.shape[0]
    key_part = keys_vals[:, 0].reshape(rows_key, heads_here, head_size)
    val_part = keys_vals[:, 1].reshape(rows_key, heads_here, head_size).astype(jnp.float32)
    scores = jnp.einsum(
        "thd,nhd->htn", queries, key_part, preferred_element_type=jnp.float32
    ) * head_size ** (-0.5)
    visible = (seg_query[:, None] == seg_key[None, :]) & (pos_query[:, None] >= pos_key[None, :])
    masked = jnp.where(visible[None], scores, NEG_FILL)
    new_max = jnp.maximum(run_max, jnp.max(masked, axis=-1))
    weights = jnp.where(visible[None], jnp.exp(masked - new_max[..., None]), 0.0)
    decay = jnp.exp(run_max - new_max)
    run_sum = run_sum * decay + jnp.sum(weights, axis=-1)
    run_acc = run_acc * decay[..., None] + jnp.einsum(
        "htn,nhd->htd", weights, val_part, precision=lax.Precision.HIGHEST
    )
    return (new_max, run_sum, run_acc)


def place_pages(pages, keys_vals, table_row, tok_index):
    rows_here = keys_vals.shape[0]
    blocks_dev = pages.shape[0]
    page_rows = pages.shape[1]
    block_ids = jnp.arange(table_row.shape[0], dtype=jnp.int32)
    wanted = tok_index * blocks_dev + 0
    source = jnp.sum(jnp.where(table_row == wanted, block_ids, 0))
    offset = source * page_rows
    inside = (offset >= 0) & (offset + page_rows <= rows_here)
    block = lax.dynamic_slice_in_dim(
        keys_vals, jnp.clip(offset, 0, rows_here - page_rows), page_rows, 0
    )
    updated = [jnp.where(inside, block, pages[0])]
    return jnp.stack(updated)


def one_layer(layer_in, seg_all, table_row, pick_rows, gains, w_qkv, w_out, w_router, w_in, w_down):
    tok_index = lax.axis_index("tok")
    tok_count = lax.axis_size("tok")
    tok_rows = layer_in.shape[0]
    width = layer_in.shape[1]
    col_width = w_qkv.shape[1] // 3
    head_count = col_width // HEAD_DIM
    experts_all = w_router.shape[1]
    local_pieces = w_in.shape[0]
    split_count = local_pieces * tok_count // experts_all
    blocks_dev = tok_rows // PAGE
    row_ids = jnp.arange(tok_rows, dtype=jnp.int32)
    pos_query = tok_index * tok_rows + row_ids
    seg_query = lax.dynamic_slice_in_dim(seg_all, tok_index * tok_rows, tok_rows)
    resid = layer_in.astype(jnp.float32)
    normed = rms_scale(resid, gains[0]).astype(jnp.bfloat16)
    projected = jnp.dot(normed, w_qkv, preferred_element_type=jnp.float32).astype(jnp.bfloat16)
    projected = projected.reshape(tok_rows, 3, col_width)
    queries = projected[:, 0].reshape(tok_rows, head_count, HEAD_DIM)
    keys_vals = projected[:, 1:]
    soft_init = (
        jnp.full((head_count, tok_rows), NEG_FILL, jnp.float32),
        jnp.zeros((head_count, tok_rows), jnp.float32),
        jnp.zeros((head_count, tok_rows, HEAD_DIM), jnp.float32),
    )
    empty_pages = jnp.zeros((blocks_dev, PAGE, 2, col_width), jnp.bfloat16)
    piece = lax.all_gather(keys_vals, "tok", axis=0, tiled=True)
    rows_key = piece.shape[0]
    step_rows = 1024
    while rows_key % step_rows != 0:
        step_rows = step_rows // 2
    turns = rows_key // step_rows

    def key_block(index, soft_now):
        start = index * step_rows
        block = lax.dynamic_slice_in_dim(piece, start, step_rows, 0)
        seg_key = lax.dynamic_slice_in_dim(seg_all, start, step_rows)
        pos_key = start + jnp.arange(step_rows, dtype=jnp.int32)
        return attend(soft_now, queries, block, seg_query, pos_query, seg_key, pos_key)

    soft_next = lax.fori_loop(0, turns, key_block, soft_init)
    pages = place_pages(empty_pages, piece, table_row, tok_index)
    run_max, run_sum, run_acc = soft_next
    context = (
        (run_acc / run_sum[..., None])
        .transpose(1, 0, 2)
        .reshape(tok_rows, col_width)
        .astype(jnp.bfloat16)
    )
    attn_part = jnp.dot(context, w_out, preferred_element_type=jnp.float32)
    mid = resid + lax.psum(attn_part, "rep")
    normed_mid = rms_scale(mid, gains[1]).astype(jnp.bfloat16)
    logits = jnp.dot(normed_mid, w_router, preferred_element_type=jnp.float32)
    expert_ids = jnp.arange(experts_all, dtype=jnp.int32)
    chosen = (pick_rows[:, :, None] == expert_ids[None, None, :]).astype(jnp.int32)
    picked_logit = jnp.sum(chosen.astype(jnp.float32) * logits[:, None, :], axis=-1)
    top_logit = jnp.max(picked_logit, axis=-1, keepdims=True)
    raised = jnp.exp(picked_logit - top_logit)
    gate_vals = raised / jnp.sum(raised, axis=-1, keepdims=True)
    ordered = chosen.transpose(1, 0, 2).reshape(TOP * tok_rows, experts_all)
    slot_of = jnp.sum((jnp.cumsum(ordered, axis=0) - 1) * ordered, axis=-1)
    flat_slot = pick_rows.T.reshape(TOP * tok_rows) * CAP + slot_of
    slot_ids = jnp.arange(experts_all * CAP, dtype=jnp.int32)
    hits = (flat_slot[:, None] == slot_ids[None, :]).astype(jnp.int32)
    hits = jnp.sum(hits.reshape(TOP, tok_rows, experts_all * CAP), axis=0).astype(jnp.bfloat16)
    dispatch = lax.dot_general(
        hits, normed_mid, (((0,), (0,)), ((), ())), preferred_element_type=jnp.float32
    ).astype(jnp.bfloat16)
    copies = jnp.broadcast_to(
        dispatch.reshape(experts_all, 1, CAP, width), (experts_all, split_count, CAP, width)
    )
    copies = copies.reshape(tok_count, local_pieces, CAP, width)
    act = jnp.einsum(
        "secd,edgf->secgf",
        lax.all_to_all(copies, "tok", split_axis=0, concat_axis=0, tiled=True),
        w_in,
        preferred_element_type=jnp.float32,
    )
    hidden = (jax.nn.gelu(act[..., 0, :]) * act[..., 1, :]).astype(jnp.bfloat16)
    returned = lax.all_to_all(
        jnp.einsum("secf,efd->secd", hidden, w_down, preferred_element_type=jnp.float32).astype(
            jnp.bfloat16
        ),
        "tok",
        split_axis=0,
        concat_axis=0,
        tiled=True,
    )
    summed = jnp.sum(
        returned.reshape(experts_all, split_count, CAP, width).astype(jnp.float32), axis=1
    )
    summed = summed.reshape(experts_all * CAP, width)
    gathered = jnp.take(summed, flat_slot, axis=0).reshape(TOP, tok_rows, width)
    expert_local = jnp.sum(gate_vals.T[:, :, None] * gathered, axis=0)
    expert_total = lax.psum(expert_local, "rep")
    layer_result = (mid + expert_total).astype(jnp.bfloat16)
    return (layer_result, pages)


def per_device(
    inputs,
    segment_ids,
    picks,
    page_table,
    norm_gains,
    attn_qkv,
    attn_out,
    router,
    expert_in,
    expert_out,
):
    section_index = lax.axis_index("section")
    is_first = section_index == 0
    width = inputs.shape[2]
    own = (
        norm_gains[0],
        attn_qkv[0].reshape(width, -1),
        attn_out[0],
        router[0],
        expert_in[0],
        expert_out[0],
    )
    swap = [(0, 1), (1, 0)]
    other = tuple((lax.ppermute(w, "section", swap) for w in own))
    weights_of = [
        tuple((jnp.where(is_first, a, b) for a, b in zip(own, other))),
        tuple((jnp.where(is_first, b, a) for a, b in zip(own, other))),
    ]
    micro = section_index
    hidden = lax.dynamic_index_in_dim(inputs, micro, 0, keepdims=False)
    seg_all = lax.dynamic_index_in_dim(segment_ids, micro, 0, keepdims=False)
    table_row = lax.dynamic_index_in_dim(page_table, micro, 0, keepdims=False)
    pick_rows = lax.dynamic_index_in_dim(picks, micro, 0, keepdims=False)
    results = []
    for layer in range(2):
        hidden, pages = one_layer(hidden, seg_all, table_row, pick_rows, *weights_of[layer])
        results.append((hidden, pages))
    (res0, pages0), (res1, pages1) = results
    got0 = lax.ppermute(res0, "section", [(1, 0)])
    gotp0 = lax.ppermute(pages0, "section", [(1, 0)])
    got1 = lax.ppermute(res1, "section", [(0, 1)])
    gotp1 = lax.ppermute(pages1, "section", [(0, 1)])
    outputs = jnp.where(is_first, jnp.stack([res0, got0]), jnp.stack([got1, res1]))
    page_out = jnp.where(is_first, jnp.stack([pages0, gotp0]), jnp.stack([gotp1, pages1]))
    return (outputs[None], page_out[None])


def solution(mesh):
    return jax.shard_map(
        per_device,
        mesh=mesh,
        in_specs=(
            P(None, "tok", None),
            P(),
            P(None, "tok", None),
            P(),
            P("section", None, None),
            P("section", None, None, "rep"),
            P("section", "rep", None),
            P("section", None, None),
            P("section", "tok", None, None, "rep"),
            P("section", "tok", "rep", None),
        ),
        out_specs=(P("section", None, "tok", None), P("section", None, "tok", None, None, "rep")),
        check_vma=False,
    )
```

profile of v0, /device:TPU:1, one launch (start us, length us, event | category | flops | bytes accessed | tf_op | source)
XLA Modules:
  0.0 634.5 jit_solution(9774270104577038417)
XLA Ops:
  7.2 1.8 copy.55
  9.0 3.3 collective-permute-start.1
  12.6 2.9 collective-permute-done
  15.5 2.1 fusion.48
  19.5 79.9 %all-gather.3.cloned.1.call-done = bf16[4096,2,256]{0,2,1:T(8,128)(2,1)} async-done(((bf16[128,2,256]{0,2,1:T(8,128)(2,1)}), bf16[4096,2,256]{0,2,1:T(8,128)(2,1)}) %all-gather.3.cloned.1.call-update) | async-done | bytes 4194320 | tf_op jit(solution)/shard_map/all_gather | solution.py:87
  99.4 17.1 %while.36 = (s32[]{:T(128)}, f32[4,128]{1,0:T(4,128)S(1)}, f32[4,128]{1,0:T(4,128)S(1)}, f32[4,128,64]{1,2,0:T(8,128)S(1)}, s32[128]{0:T(128)S(1)}, /*index=5*/s...) while((s32[]{:T(128)}, f32[4,128]{1,0:T(4,128)S(1)}, ...), condition=%wide.region_4.5_spmd.clone, body=%wide.region_1.4_spmd.clone.sunk | while | flops 476548736 | bytes 10344167 | solution.py:101
  99.7 1.3 constant_dynamic-slice_fusion.9
  102.2 1.4 fusion.180
  104.0 1.3 constant_dynamic-slice_fusion.9
  106.5 1.4 fusion.180
  108.3 1.3 constant_dynamic-slice_fusion.9
  110.8 1.4 fusion.180
  112.6 1.3 constant_dynamic-slice_fusion.9
  115.1 1.4 fusion.180
  116.6 1.1 fusion.86
  118.0 49.1 %all-reduce.5.cloned.1.call-done = f32[128,1024]{1,0:T(8,128)} async-done(((f32[128,1024]{1,0:T(8,128)}), f32[128,1024]{1,0:T(8,128)}) %all-reduce.5.cloned.1.call-update) | async-done | bytes 524304 | tf_op jit(solution)/shard_map/psum | solution.py:111
  167.2 1.2 multiply_reduce_fusion.3
  168.4 1.2 multiply_convert_fusion.1
  170.0 1.4 broadcast_in_dim.165
  171.5 9.7 %all-to-all-start = ((bf16[32,1,20,1024]{3,2,1,0:T(8,128)(2,1)}), bf16[32,1,20,1024]{3,2,1,0:T(8,128)(2,1)S(1)}, u32[]{:S(2)}, u32[]{:S(2)}) async-start(bf16[32,1,20,1024]{3,2,1,0:T(8,128)(2,1)} %bitcast.29), calls=%async_computation | async-start | bytes 3145728 | tf_op jit(solution)/shard_map/all_to_all | solution.py:135
  181.2 3.2 collective-permute-start.5
  184.7 2.9 collective-permute-done.5
  187.6 28.6 %all-to-all-done = bf16[32,1,20,1024]{3,2,1,0:T(8,128)(2,1)S(1)} async-done(((bf16[32,1,20,1024]{3,2,1,0:T(8,128)(2,1)}), bf16[32,1,20,1024]{3,2,1,0:T(8,128)(2,1)S(1)}, u32[]{:S(2)}, u32[]{:S(2)}) %all-to-all-start) | async-done | bytes 1310752 | tf_op jit(solution)/shard_map/all_to_all | solution.py:135
  216.2 3.6 convolution_bitcast_fusion.1
  219.8 2.3 fusion.42
  222.1 2.0 copy.59
  224.1 7.5 %all-to-all-start.1 = ((bf16[32,1,20,1024]{3,2,1,0:T(8,128)(2,1)}), bf16[32,1,20,1024]{3,2,1,0:T(8,128)(2,1)S(1)}, u32[]{:S(2)}, u32[]{:S(2)}) async-start(bf16[32,1,20,1024]{3,2,1,0:T(8,128)(2,1)} %copy.59), calls=%async_computation.1 | async-start | bytes 3145728 | tf_op jit(solution)/shard_map/all_to_all | solution.py:140
  231.7 2.9 collective-permute-start.3
  235.6 31.5 %all-to-all-done.1 = bf16[32,1,20,1024]{3,2,1,0:T(8,128)(2,1)S(1)} async-done(((bf16[32,1,20,1024]{3,2,1,0:T(8,128)(2,1)}), bf16[32,1,20,1024]{3,2,1,0:T(8,128)(2,1)S(1)}, u32[]{:S(2)}, u32[]{:S(2)}) %all-to-all-start.1) | async-done | bytes 1310752 | tf_op jit(solution)/shard_map/all_to_all | solution.py:140
  267.7 1.1 gather_fusion
  268.9 0.9 multiply_reduce_fusion.1
  269.9 47.1 %all-reduce.7.cloned.1.call-done = f32[128,1024]{1,0:T(8,128)} async-done(((f32[128,1024]{1,0:T(8,128)}), f32[128,1024]{1,0:T(8,128)}) %all-reduce.7.cloned.1.call-update) | async-done | bytes 524304 | tf_op jit(solution)/shard_map/psum | solution.py:155
  317.0 1.2 fusion.78
  319.9 84.1 %all-gather.5.cloned.1.call-done = bf16[4096,2,256]{0,2,1:T(8,128)(2,1)} async-done(((bf16[128,2,256]{0,2,1:T(8,128)(2,1)}), bf16[4096,2,256]{0,2,1:T(8,128)(2,1)}) %all-gather.5.cloned.1.call-update) | async-done | bytes 4194320 | tf_op jit(solution)/shard_map/all_gather | solution.py:87
  404.0 17.1 %while.37 = (s32[]{:T(128)}, f32[4,128]{1,0:T(4,128)S(1)}, f32[4,128]{1,0:T(4,128)S(1)}, f32[4,128,64]{1,2,0:T(8,128)S(1)}, s32[128]{0:T(128)S(1)}, /*index=5*/s...) while((s32[]{:T(128)}, f32[4,128]{1,0:T(4,128)S(1)}, ...), condition=%wide.region_21.23_spmd.clone, body=%wide.region_18.22_spmd.clone.sunk | while | flops 476548736 | bytes 10344167 | solution.py:101
  404.4 1.3 constant_dynamic-slice_fusion.10
  406.9 1.4 fusion.187
  408.7 1.3 constant_dynamic-slice_fusion.10
  411.2 1.4 fusion.187
  413.0 1.3 constant_dynamic-slice_fusion.10
  415.4 1.4 fusion.187
  417.3 1.3 constant_dynamic-slice_fusion.10
  419.7 1.4 fusion.187
  421.2 1.1 fusion.84
  422.3 49.5 %all-reduce.9.cloned.1.call-done = f32[128,1024]{1,0:T(8,128)} async-done(((f32[128,1024]{1,0:T(8,128)}), f32[128,1024]{1,0:T(8,128)}) %all-reduce.9.cloned.1.call-update) | async-done | bytes 524304 | tf_op jit(solution)/shard_map/psum | solution.py:111
  471.8 1.2 multiply_reduce_fusion.2
  473.0 1.2 multiply_convert_fusion
  474.8 45.7 %all_to_all.20 = bf16[32,1,20,1024]{3,2,1,0:T(8,128)(2,1)S(1)} all-to-all(bf16[32,1,20,1024]{3,2,1,0:T(8,128)(2,1)S(1)} %bitcast.258), channel_id=1, replica_groups=mesh['section'=2,'tok'=32,'rep'=4] {'tok'}, dimensions={0} | all-to-all | bytes 2621440 | tf_op jit(solution)/shard_map/all_to_all | solution.py:135
  520.5 1.8 convolution_bitcast_fusion
  522.3 1.0 fusion.43
  523.4 2.0 copy.64
  525.3 6.1 all-to-all-start.3
  531.7 31.8 %all-to-all-done.3 = bf16[32,1,20,1024]{3,2,1,0:T(8,128)(2,1)S(1)} async-done(((bf16[32,1,20,1024]{3,2,1,0:T(8,128)(2,1)}), bf16[32,1,20,1024]{3,2,1,0:T(8,128)(2,1)S(1)}, u32[]{:S(2)}, u32[]{:S(2)}) %all-to-all-start.3) | async-done | bytes 1310752 | tf_op jit(solution)/shard_map/all_to_all | solution.py:140
  564.0 1.1 gather_fusion.1
  565.3 0.9 multiply_reduce_fusion
  567.5 1.1 fusion.109
  568.6 9.9 %collective-permute-start.8 = (bf16[1,128,2,256]{1,3,2,0:T(8,128)(2,1)S(1)}, bf16[1,128,2,256]{1,3,2,0:T(8,128)(2,1)S(1)}, u32[]{:S(2)}, u32[]{:S(2)}) collective-permute-start(bf16[1,128,2,256]{1,3,2,0:T(8,128)(2,1)S(1)} %get-tuple-element.462), channel_id=1, source_target_pairs={{128,0},{129,1},{130,2},{131,3},{132,4},{133,5},{134,6},{135,7},{1... | collective-permute-start | bytes 393224 | tf_op jit(solution)/shard_map/ppermute | solution.py:200
  578.5 1.3 collective-permute-start.6
  579.8 37.5 %all-reduce.11.cloned.1.call-done = f32[128,1024]{1,0:T(8,128)} async-done(((f32[128,1024]{1,0:T(8,128)}), f32[128,1024]{1,0:T(8,128)}) %all-reduce.11.cloned.1.call-update) | async-done | bytes 524304 | tf_op jit(solution)/shard_map/psum | solution.py:155
  617.3 1.1 add_convert_fusion
  618.4 1.3 collective-permute-start.7
  619.7 1.1 fusion.111
  620.8 1.3 collective-permute-start.9
  622.1 3.7 collective-permute-done.9
  (192 shorter events, 22.9 us)
Async XLA Ops:
  7.2 12.2 %copy-start = (s32[2,4096]{1,0:T(2,128)S(1)}, s32[2,4096]{1,0:T(2,128)}, u32[]{:S(2)}) copy-start(s32[2,4096]{1,0:T(2,128)} %param.17) | copy-start | bytes 98308
  7.2 5.1 copy-start.13
  7.2 5.2 copy-start.4
  7.2 92.2 %all-gather.3.cloned.1.call-start = ((), (), s32[]{:S(2)}) async-start(), calls=%async_computation.4 | async-start | bytes 4325376 | tf_op jit(solution)/shard_map/all_gather | solution.py:87
  9.0 8.7 %copy-start.10 = (bf16[1,1024,3,256]{1,3,2,0:T(8,128)(2,1)}, bf16[1,1024,3,256]{1,3,2,0:T(8,128)(2,1)S(1)}, u32[]{:S(2)}) copy-start(bf16[1,1024,3,256]{1,3,2,0:T(8,128)(2,1)S(1)} %copy.55) | copy-start | bytes 4718596
  9.0 6.5 %collective-permute-start.1 = (bf16[1024,768]{0,1:T(8,128)(2,1)S(1)}, bf16[1024,768]{0,1:T(8,128)(2,1)}, u32[]{:S(2)}, u32[]{:S(2)}) collective-permute-start(bf16[1024,768]{0,1:T(8,128)(2,1)S(1)} %bitcast.264), channel_id=1, source_target_pairs={{0,128},{128,0},{1,129},{129,1},{2,130},{130,2},{3,131},{131,3},{4... | collective-permute-start | bytes 4718600 | tf_op jit(solution)/shard_map/ppermute | solution.py:184
  12.3 3.2 collective-permute-start
  15.5 3.1 copy-start.6
  15.5 3.2 copy-start.14
  18.6 148.6 %all-reduce.5.cloned.1.call-start = ((), (), s32[]{:S(2)}) async-start(), calls=%async_computation.5 | async-start | bytes 1048576 | tf_op jit(solution)/shard_map/psum | solution.py:111
  18.6 97.9 %collective-permute-start.2 = (bf16[256,1024]{1,0:T(8,128)(2,1)S(1)}, bf16[256,1024]{1,0:T(8,128)(2,1)S(1)}, u32[]{:S(2)}, u32[]{:S(2)}) collective-permute-start(bf16[256,1024]{1,0:T(8,128)(2,1)S(1)} %bitcast.263), channel_id=1, source_target_pairs={{0,128},{128,0},{1,129},{129,1},{2,130},{130,2},{3,131},{131,3},{4... | collective-permute-start | bytes 1572872 | tf_op jit(solution)/shard_map/ppermute | solution.py:184
  116.6 51.8 %copy-start.8 = (bf16[256,1024]{1,0:T(8,128)(2,1)}, bf16[256,1024]{1,0:T(8,128)(2,1)S(1)}, u32[]{:S(2)}) copy-start(bf16[256,1024]{1,0:T(8,128)(2,1)S(1)} %collective-permute-done.2) | copy-start | bytes 1572868
  171.5 13.0 %copy-start.17 = (bf16[1,1,352,1024]{3,2,1,0:T(8,128)(2,1)S(1)}, bf16[1,1,352,1024]{3,2,1,0:T(8,128)(2,1)}, u32[]{:S(2)}) copy-start(bf16[1,1,352,1024]{3,2,1,0:T(8,128)(2,1)} %param.25) | copy-start | bytes 2162692
  171.5 44.8 %all-to-all-start = ((bf16[32,1,20,1024]{3,2,1,0:T(8,128)(2,1)}), bf16[32,1,20,1024]{3,2,1,0:T(8,128)(2,1)S(1)}, u32[]{:S(2)}, u32[]{:S(2)}) async-start(bf16[32,1,20,1024]{3,2,1,0:T(8,128)(2,1)} %bitcast.29), calls=%async_computation | async-start | bytes 3145728 | tf_op jit(solution)/shard_map/all_to_all | solution.py:135
  181.2 6.4 %collective-permute-start.5 = (bf16[1,1024,2,352]{1,3,2,0:T(8,128)(2,1)}, bf16[1,1024,2,352]{1,3,2,0:T(8,128)(2,1)}, u32[]{:S(2)}, u32[]{:S(2)}) collective-permute-start(bf16[1,1024,2,352]{1,3,2,0:T(8,128)(2,1)} %bitcast.285), channel_id=1, source_target_pairs={{0,128},{128,0},{1,129},{129,1},{2,130},{130,2},{3,131},{131,3},{4... | collective-permute-start | bytes 4325384 | tf_op jit(solution)/shard_map/ppermute | solution.py:184
  184.4 35.4 %collective-permute-start.4 = (bf16[1,352,1024]{2,1,0:T(8,128)(2,1)S(1)}, bf16[1,352,1024]{2,1,0:T(8,128)(2,1)}, u32[]{:S(2)}, u32[]{:S(2)}) collective-permute-start(bf16[1,352,1024]{2,1,0:T(8,128)(2,1)S(1)} %bitcast.286), channel_id=1, source_target_pairs={{0,128},{128,0},{1,129},{129,1},{2,130},{130,2},{3,131},{131,3},{4... | collective-permute-start | bytes 2162696 | tf_op jit(solution)/shard_map/ppermute | solution.py:184
  224.1 7.6 %copy-start.12 = (bf16[1,1024,16]{1,2,0:T(8,128)(2,1)S(1)}, bf16[1,1024,16]{1,2,0:T(8,128)(2,1)}, u32[]{:S(2)}) copy-start(bf16[1,1024,16]{1,2,0:T(8,128)(2,1)} %param.23) | copy-start | bytes 98308
  224.1 43.1 %all-to-all-start.1 = ((bf16[32,1,20,1024]{3,2,1,0:T(8,128)(2,1)}), bf16[32,1,20,1024]{3,2,1,0:T(8,128)(2,1)S(1)}, u32[]{:S(2)}, u32[]{:S(2)}) async-start(bf16[32,1,20,1024]{3,2,1,0:T(8,128)(2,1)} %copy.59), calls=%async_computation.1 | async-start | bytes 3145728 | tf_op jit(solution)/shard_map/all_to_all | solution.py:140
  231.6 85.4 %all-reduce.7.cloned.1.call-start = ((), (), s32[]{:S(2)}) async-start(), calls=%async_computation.6 | async-start | bytes 1048576 | tf_op jit(solution)/shard_map/psum | solution.py:155
  231.7 3.7 collective-permute-start.3
  268.7 48.3 %copy-start.3 = (f32[128,1024]{1,0:T(8,128)S(1)}, f32[128,1024]{1,0:T(8,128)}, u32[]{:S(2)}) copy-start(f32[128,1024]{1,0:T(8,128)} %all-reduce.5.cloned.1.call-done) | copy-start | bytes 1572868
  268.8 48.3 %copy-start.5 = (bf16[2,128,1024]{2,1,0:T(8,128)(2,1)S(1)}, bf16[2,128,1024]{2,1,0:T(8,128)(2,1)}, u32[]{:S(2)}) copy-start(bf16[2,128,1024]{2,1,0:T(8,128)(2,1)} %param.16) | copy-start | bytes 1572868
  268.9 49.3 %copy-start.11 = (bf16[1,1024,3,256]{1,3,2,0:T(8,128)(2,1)S(1)}, bf16[1,1024,3,256]{1,3,2,0:T(8,128)(2,1)}, u32[]{:S(2)}) copy-start(bf16[1,1024,3,256]{1,3,2,0:T(8,128)(2,1)} %copy-done.10) | copy-start | bytes 4718596
  269.9 134.2 %all-gather.5.cloned.1.call-start = ((), (), s32[]{:S(2)}) async-start(), calls=%async_computation.7 | async-start | bytes 4325376 | tf_op jit(solution)/shard_map/all_gather | solution.py:87
  319.8 152.0 %all-reduce.9.cloned.1.call-start = ((), (), s32[]{:S(2)}) async-start(), calls=%async_computation.8 | async-start | bytes 1048576 | tf_op jit(solution)/shard_map/psum | solution.py:111
  404.0 17.2 %copy-start.7 = (bf16[1,256,1024]{2,1,0:T(8,128)(2,1)S(1)}, bf16[1,256,1024]{2,1,0:T(8,128)(2,1)}, u32[]{:S(2)}) copy-start(bf16[1,256,1024]{2,1,0:T(8,128)(2,1)} %param.22) | copy-start | bytes 1572868
  404.0 17.2 %copy-start.9 = (bf16[256,1024]{1,0:T(8,128)(2,1)S(1)}, bf16[256,1024]{1,0:T(8,128)(2,1)}, u32[]{:S(2)}) copy-start(bf16[256,1024]{1,0:T(8,128)(2,1)} %copy-done.8) | copy-start | bytes 1572868
  474.8 45.7 %copy-start.16 = (bf16[1,1,1024,2,352]{2,4,3,1,0:T(8,128)(2,1)S(1)}, bf16[1,1,1024,2,352]{2,4,3,1,0:T(8,128)(2,1)}, u32[]{:S(2)}) copy-start(bf16[1,1,1024,2,352]{2,4,3,1,0:T(8,128)(2,1)} %param.24) | copy-start | bytes 4325380
  520.5 1.8 copy-start.18
  525.3 38.2 %all-to-all-start.3 = ((bf16[32,1,20,1024]{3,2,1,0:T(8,128)(2,1)}), bf16[32,1,20,1024]{3,2,1,0:T(8,128)(2,1)S(1)}, u32[]{:S(2)}, u32[]{:S(2)}) async-start(bf16[32,1,20,1024]{3,2,1,0:T(8,128)(2,1)} %copy.64), calls=%async_computation.3 | async-start | bytes 3145728 | tf_op jit(solution)/shard_map/all_to_all | solution.py:140
  531.4 85.8 %all-reduce.11.cloned.1.call-start = ((), (), s32[]{:S(2)}) async-start(), calls=%async_computation.9 | async-start | bytes 1048576 | tf_op jit(solution)/shard_map/psum | solution.py:155
  565.1 1.1 copy-start.15
  565.1 52.2 %copy-start.2 = (f32[128,1024]{1,0:T(8,128)S(1)}, f32[128,1024]{1,0:T(8,128)}, u32[]{:S(2)}) copy-start(f32[128,1024]{1,0:T(8,128)} %all-reduce.9.cloned.1.call-done) | copy-start | bytes 1572868
  568.6 53.5 %collective-permute-start.8 = (bf16[1,128,2,256]{1,3,2,0:T(8,128)(2,1)S(1)}, bf16[1,128,2,256]{1,3,2,0:T(8,128)(2,1)S(1)}, u32[]{:S(2)}, u32[]{:S(2)}) collective-permute-start(bf16[1,128,2,256]{1,3,2,0:T(8,128)(2,1)S(1)} %get-tuple-element.462), channel_id=1, source_target_pairs={{128,0},{129,1},{130,2},{131,3},{132,4},{133,5},{134,6},{135,7},{1... | collective-permute-start | bytes 393224 | tf_op jit(solution)/shard_map/ppermute | solution.py:200
  578.5 48.3 %collective-permute-start.6 = (bf16[128,1024]{1,0:T(8,128)(2,1)S(1)}, bf16[128,1024]{1,0:T(8,128)(2,1)S(1)}, u32[]{:S(2)}, u32[]{:S(2)}) collective-permute-start(bf16[128,1024]{1,0:T(8,128)(2,1)S(1)} %get-tuple-element.448), channel_id=1, source_target_pairs={{128,0},{129,1},{130,2},{131,3},{132,4},{133,5},{134,6},{135,7},{1... | collective-permute-start | bytes 786440 | tf_op jit(solution)/shard_map/ppermute | solution.py:199
  617.3 10.4 %copy-start.1 = (s32[2,4096]{1,0:T(2,128)S(1)}, s32[2,4096]{1,0:T(2,128)}, u32[]{:S(2)}) copy-start(s32[2,4096]{1,0:T(2,128)} %param.17) | copy-start | bytes 98308
  618.4 8.3 %collective-permute-start.7 = (bf16[128,1024]{1,0:T(8,128)(2,1)S(1)}, bf16[128,1024]{1,0:T(8,128)(2,1)S(1)}, u32[]{:S(2)}, u32[]{:S(2)}) collective-permute-start(bf16[128,1024]{1,0:T(8,128)(2,1)S(1)} %add_convert_fusion), channel_id=1, source_target_pairs={{0,128},{1,129},{2,130},{3,131},{4,132},{5,133},{6,134},{7,135},{8... | collective-permute-start | bytes 786440 | tf_op jit(solution)/shard_map/ppermute | solution.py:201
  620.8 5.0 collective-permute-start.9
Sparse Core Ops, SparseCore 0:
  18.7 80.6 all-gather.2
  117.8 49.3 all-reduce.4
  270.0 46.9 all-reduce.6
  319.9 84.0 all-gather.4
  422.4 49.3 all-reduce.8
  566.3 50.8 all-reduce.10
where the time goes:
time: 636 us; the launch traced here: 634 us
  waiting for transfers between devices  450 us (71%)
  starting transfers between devices  47.2 us (7%)
  blocking collectives  45.7 us (7%)
  matrix products  30.8 us (5%)
  local copies, waits for them, and re-layouts  23.3 us (4%)
  other arithmetic  22 us (3%)
  between operations  15.4 us (2%)
    all_gather x2, waiting for transfers between devices, one_layer(): piece = lax.all_gather(keys_vals, 'tok', axis=0, tiled=True)  164 us
    psum x2, waiting for transfers between devices, one_layer(): mid = resid + lax.psum(attn_part, 'rep')  98.6 us
    psum x2, waiting for transfers between devices, one_layer(): expert_total = lax.psum(expert_local, 'rep')  84.6 us
    all_to_all x2, waiting for transfers between devices, one_layer(): lax.all_to_all(jnp.einsum('secf,efd->secd', hidden, w_down, preferred_ele...  63.3 us
    all_to_all x1, blocking collectives, one_layer(): lax.all_to_all(copies, 'tok', split_axis=0, concat_axis=0, tiled=True)  45.7 us
    all_to_all x1, waiting for transfers between devices, one_layer(): lax.all_to_all(copies, 'tok', split_axis=0, concat_axis=0, tiled=True)  28.6 us
    all_to_all x2, starting transfers between devices, one_layer(): lax.all_to_all(jnp.einsum('secf,efd->secd', hidden, w_down, preferred_ele...  13.6 us
  transfers between devices with their start and end apart: 19, of which 13 were waited for; matrix products, arithmetic and copies ran while one was open for 4% of the time, Pallas kernels for 0%

commit v1 on v0

--- a/solution.py
+++ b/solution.py
@@ -152,7 +152,7 @@
     summed = summed.reshape(experts_all * CAP, width)
     gathered = jnp.take(summed, flat_slot, axis=0).reshape(TOP, tok_rows, width)
     expert_local = jnp.sum(gate_vals.T[:, :, None] * gathered, axis=0)
-    expert_total = lax.psum(expert_local, "rep")
+    expert_total = jnp.sum(lax.all_gather(expert_local, "rep"), axis=0)
     layer_result = (mid + expert_total).astype(jnp.bfloat16)
     return (layer_result, pages)
 

time: 636 us -> 607 us (0.954)
  waiting for transfers between devices: 450 us -> 421 us
    psum x2 -> x0, waiting for transfers between devices: 84.6 us -> none  [one_layer(): expert_total = lax.psum(expert_local, 'rep')]
    all_gather x0 -> x2, waiting for transfers between devices: none -> 58.6 us  [one_layer(): expert_total = jnp.sum(lax.all_gather(expert_local, 'rep'), axis=0)]
  transfers between devices with their start and end apart: 19 -> 19, of which waited for: 13 -> 13; matrix products, arithmetic and copies ran while one was open for 4% -> 5% of each run, Pallas kernels for 0% -> 0%
where the time goes in v1:
time: 607 us; the launch traced here: 606 us
  waiting for transfers between devices  421 us (69%)
  starting transfers between devices  46.3 us (8%)
  blocking collectives  45.7 us (8%)
  matrix products  30.6 us (5%)
  other arithmetic  23.6 us (4%)
  local copies, waits for them, and re-layouts  23.2 us (4%)
  between operations  15.5 us (3%)
    all_gather x2, waiting for transfers between devices, one_layer(): piece = lax.all_gather(keys_vals, 'tok', axis=0, tiled=True)  162 us
    psum x2, waiting for transfers between devices, one_layer(): mid = resid + lax.psum(attn_part, 'rep')  98.7 us
    all_to_all x2, waiting for transfers between devices, one_layer(): lax.all_to_all(jnp.einsum('secf,efd->secd', hidden, w_down, preferred_ele...  64.5 us
    all_gather x2, waiting for transfers between devices, one_layer(): expert_total = jnp.sum(lax.all_gather(expert_local, 'rep'), axis=0)  58.6 us
    all_to_all x1, blocking collectives, one_layer(): lax.all_to_all(copies, 'tok', split_axis=0, concat_axis=0, tiled=True)  45.7 us
    all_to_all x1, waiting for transfers between devices, one_layer(): lax.all_to_all(copies, 'tok', split_axis=0, concat_axis=0, tiled=True)  28.6 us
    all_to_all x2, starting transfers between devices, one_layer(): lax.all_to_all(jnp.einsum('secf,efd->secd', hidden, w_down, preferred_ele...  13.6 us
  transfers between devices with their start and end apart: 19, of which 13 were waited for; matrix products, arithmetic and copies ran while one was open for 5% of the time, Pallas kernels for 0%

profile of v1, /device:TPU:1, one launch (start us, length us, event | category | flops | bytes accessed | tf_op | source)
XLA Modules:
  0.0 606.0 jit_solution(3488729540491406978)
XLA Ops:
  7.2 1.8 copy.55
  9.0 3.3 collective-permute-start.1
  12.6 2.9 collective-permute-done
  15.5 2.1 fusion.48
  19.5 79.9 %all-gather.7.cloned.1.call-done = bf16[4096,2,256]{0,2,1:T(8,128)(2,1)} async-done(((bf16[128,2,256]{0,2,1:T(8,128)(2,1)}), bf16[4096,2,256]{0,2,1:T(8,128)(2,1)}) %all-gather.7.cloned.1.call-update) | async-done | bytes 4194320 | tf_op jit(solution)/shard_map/all_gather | solution.py:87
  99.4 17.1 %while.36 = (s32[]{:T(128)}, f32[4,128]{1,0:T(4,128)S(1)}, f32[4,128]{1,0:T(4,128)S(1)}, f32[4,128,64]{1,2,0:T(8,128)S(1)}, s32[128]{0:T(128)S(1)}, /*index=5*/s...) while((s32[]{:T(128)}, f32[4,128]{1,0:T(4,128)S(1)}, ...), condition=%wide.region_4.5_spmd.clone, body=%wide.region_1.4_spmd.clone.sunk | while | flops 476548736 | bytes 10344167 | solution.py:101
  99.7 1.3 constant_dynamic-slice_fusion.9
  102.2 1.4 fusion.180
  104.0 1.3 constant_dynamic-slice_fusion.9
  106.5 1.4 fusion.180
  108.3 1.3 constant_dynamic-slice_fusion.9
  110.8 1.4 fusion.180
  112.6 1.3 constant_dynamic-slice_fusion.9
  115.1 1.4 fusion.180
  116.6 1.1 fusion.86
  118.1 49.1 %all-reduce.3.cloned.1.call-done = f32[128,1024]{1,0:T(8,128)} async-done(((f32[128,1024]{1,0:T(8,128)}), f32[128,1024]{1,0:T(8,128)}) %all-reduce.3.cloned.1.call-update) | async-done | bytes 524304 | tf_op jit(solution)/shard_map/psum | solution.py:111
  167.2 1.2 multiply_reduce_fusion.3
  168.4 1.2 multiply_convert_fusion.1
  170.0 1.4 broadcast_in_dim.165
  171.4 9.7 %all-to-all-start = ((bf16[32,1,20,1024]{3,2,1,0:T(8,128)(2,1)}), bf16[32,1,20,1024]{3,2,1,0:T(8,128)(2,1)S(1)}, u32[]{:S(2)}, u32[]{:S(2)}) async-start(bf16[32,1,20,1024]{3,2,1,0:T(8,128)(2,1)} %bitcast.29), calls=%async_computation | async-start | bytes 3145728 | tf_op jit(solution)/shard_map/all_to_all | solution.py:135
  181.1 3.2 collective-permute-start.5
  184.7 2.9 collective-permute-done.5
  187.6 28.6 %all-to-all-done = bf16[32,1,20,1024]{3,2,1,0:T(8,128)(2,1)S(1)} async-done(((bf16[32,1,20,1024]{3,2,1,0:T(8,128)(2,1)}), bf16[32,1,20,1024]{3,2,1,0:T(8,128)(2,1)S(1)}, u32[]{:S(2)}, u32[]{:S(2)}) %all-to-all-start) | async-done | bytes 1310752 | tf_op jit(solution)/shard_map/all_to_all | solution.py:135
  216.2 3.6 convolution_bitcast_fusion.1
  219.7 2.1 fusion.42
  221.9 1.9 copy.59
  223.8 7.5 %all-to-all-start.1 = ((bf16[32,1,20,1024]{3,2,1,0:T(8,128)(2,1)}), bf16[32,1,20,1024]{3,2,1,0:T(8,128)(2,1)S(1)}, u32[]{:S(2)}, u32[]{:S(2)}) async-start(bf16[32,1,20,1024]{3,2,1,0:T(8,128)(2,1)} %copy.59), calls=%async_computation.1 | async-start | bytes 3145728 | tf_op jit(solution)/shard_map/all_to_all | solution.py:140
  231.3 2.0 collective-permute-start.3
  234.4 32.7 %all-to-all-done.1 = bf16[32,1,20,1024]{3,2,1,0:T(8,128)(2,1)S(1)} async-done(((bf16[32,1,20,1024]{3,2,1,0:T(8,128)(2,1)}), bf16[32,1,20,1024]{3,2,1,0:T(8,128)(2,1)S(1)}, u32[]{:S(2)}, u32[]{:S(2)}) %all-to-all-start.1) | async-done | bytes 1310752 | tf_op jit(solution)/shard_map/all_to_all | solution.py:140
  267.7 1.1 gather_fusion
  268.9 0.9 multiply_reduce_fusion.1
  269.9 33.9 %all-gather.11.cloned.1.call-done = f32[512,1024]{1,0:T(8,128)} async-done(((f32[128,1024]{1,0:T(8,128)}), f32[512,1024]{1,0:T(8,128)}) %all-gather.11.cloned.1.call-update) | async-done | bytes 2097168 | tf_op jit(solution)/shard_map/all_gather | solution.py:155
  303.8 1.9 reduce_sum.202
  307.6 81.6 %all-gather.9.cloned.1.call-done = bf16[4096,2,256]{0,2,1:T(8,128)(2,1)} async-done(((bf16[128,2,256]{0,2,1:T(8,128)(2,1)}), bf16[4096,2,256]{0,2,1:T(8,128)(2,1)}) %all-gather.9.cloned.1.call-update) | async-done | bytes 4194320 | tf_op jit(solution)/shard_map/all_gather | solution.py:87
  389.2 17.1 %while.37 = (s32[]{:T(128)}, f32[4,128]{1,0:T(4,128)S(1)}, f32[4,128]{1,0:T(4,128)S(1)}, f32[4,128,64]{1,2,0:T(8,128)S(1)}, s32[128]{0:T(128)S(1)}, /*index=5*/s...) while((s32[]{:T(128)}, f32[4,128]{1,0:T(4,128)S(1)}, ...), condition=%wide.region_21.23_spmd.clone, body=%wide.region_18.22_spmd.clone.sunk | while | flops 476548736 | bytes 10344167 | solution.py:101
  389.6 1.3 constant_dynamic-slice_fusion.10
  392.1 1.4 fusion.187
  393.9 1.3 constant_dynamic-slice_fusion.10
  396.4 1.4 fusion.187
  398.2 1.3 constant_dynamic-slice_fusion.10
  400.7 1.4 fusion.187
  402.5 1.3 constant_dynamic-slice_fusion.10
  404.9 1.4 fusion.187
  406.4 1.1 fusion.84
  407.5 49.5 %all-reduce.5.cloned.1.call-done = f32[128,1024]{1,0:T(8,128)} async-done(((f32[128,1024]{1,0:T(8,128)}), f32[128,1024]{1,0:T(8,128)}) %all-reduce.5.cloned.1.call-update) | async-done | bytes 524304 | tf_op jit(solution)/shard_map/psum | solution.py:111
  457.1 1.2 multiply_reduce_fusion.2
  458.3 1.2 multiply_convert_fusion
  460.1 45.7 %all_to_all.20 = bf16[32,1,20,1024]{3,2,1,0:T(8,128)(2,1)S(1)} all-to-all(bf16[32,1,20,1024]{3,2,1,0:T(8,128)(2,1)S(1)} %bitcast.260), channel_id=1, replica_groups=mesh['section'=2,'tok'=32,'rep'=4] {'tok'}, dimensions={0} | all-to-all | bytes 2621440 | tf_op jit(solution)/shard_map/all_to_all | solution.py:135
  505.8 1.8 convolution_bitcast_fusion
  507.6 1.0 fusion.43
  508.7 2.0 copy.64
  510.6 6.1 %all-to-all-start.3 = ((bf16[32,1,20,1024]{3,2,1,0:T(8,128)(2,1)}), bf16[32,1,20,1024]{3,2,1,0:T(8,128)(2,1)S(1)}, u32[]{:S(2)}, u32[]{:S(2)}) async-start(bf16[32,1,20,1024]{3,2,1,0:T(8,128)(2,1)} %copy.64), calls=%async_computation.3 | async-start | bytes 3145728 | tf_op jit(solution)/shard_map/all_to_all | solution.py:140
  517.0 31.8 %all-to-all-done.3 = bf16[32,1,20,1024]{3,2,1,0:T(8,128)(2,1)S(1)} async-done(((bf16[32,1,20,1024]{3,2,1,0:T(8,128)(2,1)}), bf16[32,1,20,1024]{3,2,1,0:T(8,128)(2,1)S(1)}, u32[]{:S(2)}, u32[]{:S(2)}) %all-to-all-start.3) | async-done | bytes 1310752 | tf_op jit(solution)/shard_map/all_to_all | solution.py:140
  549.3 1.1 gather_fusion.1
  550.5 0.9 multiply_reduce_fusion
  552.8 1.1 fusion.109
  553.9 9.9 %collective-permute-start.8 = (bf16[1,128,2,256]{1,3,2,0:T(8,128)(2,1)S(1)}, bf16[1,128,2,256]{1,3,2,0:T(8,128)(2,1)S(1)}, u32[]{:S(2)}, u32[]{:S(2)}) collective-permute-start(bf16[1,128,2,256]{1,3,2,0:T(8,128)(2,1)S(1)} %get-tuple-element.462), channel_id=1, source_target_pairs={{128,0},{129,1},{130,2},{131,3},{132,4},{133,5},{134,6},{135,7},{1... | collective-permute-start | bytes 393224 | tf_op jit(solution)/shard_map/ppermute | solution.py:200
  563.7 1.3 collective-permute-start.6
  565.1 24.7 %all-gather.13.cloned.1.call-done = f32[512,1024]{1,0:T(8,128)} async-done(((f32[128,1024]{1,0:T(8,128)}), f32[512,1024]{1,0:T(8,128)}) %all-gather.13.cloned.1.call-update) | async-done | bytes 2097168 | tf_op jit(solution)/shard_map/all_gather | solution.py:155
  589.7 1.8 reduce_sum.209
  591.7 1.3 collective-permute-start.7
  593.0 1.1 fusion.111
  594.0 1.3 collective-permute-start.9
  595.3 1.9 collective-permute-done.9
  (198 shorter events, 23.2 us)
Async XLA Ops:
  7.2 12.2 %copy-start = (s32[2,4096]{1,0:T(2,128)S(1)}, s32[2,4096]{1,0:T(2,128)}, u32[]{:S(2)}) copy-start(s32[2,4096]{1,0:T(2,128)} %param.17) | copy-start | bytes 98308
  7.2 5.1 copy-start.15
  7.2 5.2 copy-start.4
  7.2 92.2 %all-gather.7.cloned.1.call-start = ((), (), s32[]{:S(2)}) async-start(), calls=%async_computation.4 | async-start | bytes 4325376 | tf_op jit(solution)/shard_map/all_gather | solution.py:87
  9.0 8.7 %copy-start.10 = (bf16[1,1024,3,256]{1,3,2,0:T(8,128)(2,1)}, bf16[1,1024,3,256]{1,3,2,0:T(8,128)(2,1)S(1)}, u32[]{:S(2)}) copy-start(bf16[1,1024,3,256]{1,3,2,0:T(8,128)(2,1)S(1)} %copy.55) | copy-start | bytes 4718596
  9.0 6.5 %collective-permute-start.1 = (bf16[1024,768]{0,1:T(8,128)(2,1)S(1)}, bf16[1024,768]{0,1:T(8,128)(2,1)}, u32[]{:S(2)}, u32[]{:S(2)}) collective-permute-start(bf16[1024,768]{0,1:T(8,128)(2,1)S(1)} %bitcast.268), channel_id=1, source_target_pairs={{0,128},{128,0},{1,129},{129,1},{2,130},{130,2},{3,131},{131,3},{4... | collective-permute-start | bytes 4718600 | tf_op jit(solution)/shard_map/ppermute | solution.py:184
  12.3 3.2 collective-permute-start
  15.5 3.1 copy-start.6
  15.5 3.2 copy-start.16
  18.6 148.6 %all-reduce.3.cloned.1.call-start = ((), (), s32[]{:S(2)}) async-start(), calls=%async_computation.5 | async-start | bytes 1048576 | tf_op jit(solution)/shard_map/psum | solution.py:111
  18.6 97.9 %collective-permute-start.2 = (bf16[256,1024]{1,0:T(8,128)(2,1)S(1)}, bf16[256,1024]{1,0:T(8,128)(2,1)S(1)}, u32[]{:S(2)}, u32[]{:S(2)}) collective-permute-start(bf16[256,1024]{1,0:T(8,128)(2,1)S(1)} %bitcast.267), channel_id=1, source_target_pairs={{0,128},{128,0},{1,129},{129,1},{2,130},{130,2},{3,131},{131,3},{4... | collective-permute-start | bytes 1572872 | tf_op jit(solution)/shard_map/ppermute | solution.py:184
  116.6 51.8 %copy-start.8 = (bf16[256,1024]{1,0:T(8,128)(2,1)}, bf16[256,1024]{1,0:T(8,128)(2,1)S(1)}, u32[]{:S(2)}) copy-start(bf16[256,1024]{1,0:T(8,128)(2,1)S(1)} %collective-permute-done.2) | copy-start | bytes 1572868
  118.0 51.5 %copy-start.12 = (s32[128,320]{0,1:T(8,128)}, s32[128,320]{0,1:T(8,128)S(1)}, u32[]{:S(2)}) copy-start(s32[128,320]{0,1:T(8,128)S(1)} %convert_reduce_fusion.2) | copy-start | bytes 491524
  171.4 13.0 %copy-start.19 = (bf16[1,1,352,1024]{3,2,1,0:T(8,128)(2,1)S(1)}, bf16[1,1,352,1024]{3,2,1,0:T(8,128)(2,1)}, u32[]{:S(2)}) copy-start(bf16[1,1,352,1024]{3,2,1,0:T(8,128)(2,1)} %param.25) | copy-start | bytes 2162692
  171.4 44.8 %all-to-all-start = ((bf16[32,1,20,1024]{3,2,1,0:T(8,128)(2,1)}), bf16[32,1,20,1024]{3,2,1,0:T(8,128)(2,1)S(1)}, u32[]{:S(2)}, u32[]{:S(2)}) async-start(bf16[32,1,20,1024]{3,2,1,0:T(8,128)(2,1)} %bitcast.29), calls=%async_computation | async-start | bytes 3145728 | tf_op jit(solution)/shard_map/all_to_all | solution.py:135
  181.1 6.4 %collective-permute-start.5 = (bf16[1,1024,2,352]{1,3,2,0:T(8,128)(2,1)}, bf16[1,1024,2,352]{1,3,2,0:T(8,128)(2,1)}, u32[]{:S(2)}, u32[]{:S(2)}) collective-permute-start(bf16[1,1024,2,352]{1,3,2,0:T(8,128)(2,1)} %bitcast.289), channel_id=1, source_target_pairs={{0,128},{128,0},{1,129},{129,1},{2,130},{130,2},{3,131},{131,3},{4... | collective-permute-start | bytes 4325384 | tf_op jit(solution)/shard_map/ppermute | solution.py:184
  184.4 35.4 %collective-permute-start.4 = (bf16[1,352,1024]{2,1,0:T(8,128)(2,1)S(1)}, bf16[1,352,1024]{2,1,0:T(8,128)(2,1)}, u32[]{:S(2)}, u32[]{:S(2)}) collective-permute-start(bf16[1,352,1024]{2,1,0:T(8,128)(2,1)S(1)} %bitcast.290), channel_id=1, source_target_pairs={{0,128},{128,0},{1,129},{129,1},{2,130},{130,2},{3,131},{131,3},{4... | collective-permute-start | bytes 2162696 | tf_op jit(solution)/shard_map/ppermute | solution.py:184
  223.8 7.6 %copy-start.14 = (bf16[1,1024,16]{1,2,0:T(8,128)(2,1)S(1)}, bf16[1,1024,16]{1,2,0:T(8,128)(2,1)}, u32[]{:S(2)}) copy-start(bf16[1,1024,16]{1,2,0:T(8,128)(2,1)} %param.23) | copy-start | bytes 98308
  223.8 43.4 %all-to-all-start.1 = ((bf16[32,1,20,1024]{3,2,1,0:T(8,128)(2,1)}), bf16[32,1,20,1024]{3,2,1,0:T(8,128)(2,1)S(1)}, u32[]{:S(2)}, u32[]{:S(2)}) async-start(bf16[32,1,20,1024]{3,2,1,0:T(8,128)(2,1)} %copy.59), calls=%async_computation.1 | async-start | bytes 3145728 | tf_op jit(solution)/shard_map/all_to_all | solution.py:140
  231.3 72.6 %all-gather.11.cloned.1.call-start = ((), (), s32[]{:S(2)}) async-start(), calls=%async_computation.8 | async-start | bytes 2621440 | tf_op jit(solution)/shard_map/all_gather | solution.py:155
  231.3 2.8 collective-permute-start.3
  269.8 36.0 %copy-start.3 = (f32[128,1024]{1,0:T(8,128)S(1)}, f32[128,1024]{1,0:T(8,128)}, u32[]{:S(2)}) copy-start(f32[128,1024]{1,0:T(8,128)} %all-reduce.3.cloned.1.call-done) | copy-start | bytes 1572868
  269.8 36.0 %copy-start.5 = (bf16[2,128,1024]{2,1,0:T(8,128)(2,1)S(1)}, bf16[2,128,1024]{2,1,0:T(8,128)(2,1)}, u32[]{:S(2)}) copy-start(bf16[2,128,1024]{2,1,0:T(8,128)(2,1)} %param.16) | copy-start | bytes 1572868
  269.8 119.4 %all-gather.9.cloned.1.call-start = ((), (), s32[]{:S(2)}) async-start(), calls=%async_computation.6 | async-start | bytes 4325376 | tf_op jit(solution)/shard_map/all_gather | solution.py:87
  303.8 2.1 copy-start.11
  307.5 149.6 %all-reduce.5.cloned.1.call-start = ((), (), s32[]{:S(2)}) async-start(), calls=%async_computation.7 | async-start | bytes 1048576 | tf_op jit(solution)/shard_map/psum | solution.py:111
  389.2 17.2 %copy-start.7 = (bf16[1,256,1024]{2,1,0:T(8,128)(2,1)S(1)}, bf16[1,256,1024]{2,1,0:T(8,128)(2,1)}, u32[]{:S(2)}) copy-start(bf16[1,256,1024]{2,1,0:T(8,128)(2,1)} %param.22) | copy-start | bytes 1572868
  389.2 17.2 %copy-start.9 = (bf16[256,1024]{1,0:T(8,128)(2,1)S(1)}, bf16[256,1024]{1,0:T(8,128)(2,1)}, u32[]{:S(2)}) copy-start(bf16[256,1024]{1,0:T(8,128)(2,1)} %copy-done.8) | copy-start | bytes 1572868
  406.4 53.0 %copy-start.13 = (s32[128,320]{0,1:T(8,128)S(1)}, s32[128,320]{0,1:T(8,128)}, u32[]{:S(2)}) copy-start(s32[128,320]{0,1:T(8,128)} %copy-done.12) | copy-start | bytes 491524
  460.1 45.7 %copy-start.18 = (bf16[1,1,1024,2,352]{2,4,3,1,0:T(8,128)(2,1)S(1)}, bf16[1,1,1024,2,352]{2,4,3,1,0:T(8,128)(2,1)}, u32[]{:S(2)}) copy-start(bf16[1,1,1024,2,352]{2,4,3,1,0:T(8,128)(2,1)} %param.24) | copy-start | bytes 4325380
  505.8 1.8 copy-start.20
  510.6 38.2 %all-to-all-start.3 = ((bf16[32,1,20,1024]{3,2,1,0:T(8,128)(2,1)}), bf16[32,1,20,1024]{3,2,1,0:T(8,128)(2,1)S(1)}, u32[]{:S(2)}, u32[]{:S(2)}) async-start(bf16[32,1,20,1024]{3,2,1,0:T(8,128)(2,1)} %copy.64), calls=%async_computation.3 | async-start | bytes 3145728 | tf_op jit(solution)/shard_map/all_to_all | solution.py:140
  516.7 73.0 %all-gather.13.cloned.1.call-start = ((), (), s32[]{:S(2)}) async-start(), calls=%async_computation.9 | async-start | bytes 2621440 | tf_op jit(solution)/shard_map/all_gather | solution.py:155
  550.4 1.1 copy-start.17
  551.5 40.1 %copy-start.2 = (f32[128,1024]{1,0:T(8,128)S(1)}, f32[128,1024]{1,0:T(8,128)}, u32[]{:S(2)}) copy-start(f32[128,1024]{1,0:T(8,128)} %all-reduce.5.cloned.1.call-done) | copy-start | bytes 1572868
  553.9 41.5 %collective-permute-start.8 = (bf16[1,128,2,256]{1,3,2,0:T(8,128)(2,1)S(1)}, bf16[1,128,2,256]{1,3,2,0:T(8,128)(2,1)S(1)}, u32[]{:S(2)}, u32[]{:S(2)}) collective-permute-start(bf16[1,128,2,256]{1,3,2,0:T(8,128)(2,1)S(1)} %get-tuple-element.462), channel_id=1, source_target_pairs={{128,0},{129,1},{130,2},{131,3},{132,4},{133,5},{134,6},{135,7},{1... | collective-permute-start | bytes 393224 | tf_op jit(solution)/shard_map/ppermute | solution.py:200
  563.7 34.5 %collective-permute-start.6 = (bf16[128,1024]{1,0:T(8,128)(2,1)S(1)}, bf16[128,1024]{1,0:T(8,128)(2,1)S(1)}, u32[]{:S(2)}, u32[]{:S(2)}) collective-permute-start(bf16[128,1024]{1,0:T(8,128)(2,1)S(1)} %get-tuple-element.448), channel_id=1, source_target_pairs={{128,0},{129,1},{130,2},{131,3},{132,4},{133,5},{134,6},{135,7},{1... | collective-permute-start | bytes 786440 | tf_op jit(solution)/shard_map/ppermute | solution.py:199
  591.5 7.6 %copy-start.1 = (s32[2,4096]{1,0:T(2,128)S(1)}, s32[2,4096]{1,0:T(2,128)}, u32[]{:S(2)}) copy-start(s32[2,4096]{1,0:T(2,128)} %param.17) | copy-start | bytes 98308
  591.7 6.6 %collective-permute-start.7 = (bf16[128,1024]{1,0:T(8,128)(2,1)S(1)}, bf16[128,1024]{1,0:T(8,128)(2,1)S(1)}, u32[]{:S(2)}, u32[]{:S(2)}) collective-permute-start(bf16[128,1024]{1,0:T(8,128)(2,1)S(1)} %add_convert_fusion), channel_id=1, source_target_pairs={{0,128},{1,129},{2,130},{3,131},{4,132},{5,133},{6,134},{7,135},{8... | collective-permute-start | bytes 786440 | tf_op jit(solution)/shard_map/ppermute | solution.py:201
  594.0 3.3 collective-permute-start.9
Sparse Core Ops, SparseCore 0:
  18.7 80.6 all-gather.6
  117.8 49.3 all-reduce.2
  270.0 33.8 all-gather.10
  307.6 81.5 all-gather.8
  407.7 49.3 all-reduce.4
  551.6 38.0 all-gather.12
